TPU v7x, 256 devices: a whole 4x4x8 slice. The times are simulated.
256 devices in a mesh: ctx: 32 (over y, x, core), head: 8 (over z).
Axes of the slice: x: 4, y: 4, z: 8, core: 2. Of those that a mesh axis runs over, the one named last changes fastest.
Arguments:
- queries: bfloat16 [8192, 4096], P('ctx', 'head'), may hold values from -6 to 6
- key_rows: bfloat16 [8192, 4096], P('ctx', 'head'), may hold values from -6 to 6
- values: bfloat16 [8192, 4096], P('ctx', 'head'), may hold values from -6 to 6
- log_decay: float32 [8192, 32], P('ctx', 'head'), may hold values from 0 to 1, as said below
- head_gain: bfloat16 [4096], P('head'), may hold values from 0.099609375 to 1.8984375
- out_weight: bfloat16 [3072, 4096], P('ctx', 'head'), may hold values from -0.09375 to 0.09375
- residual: bfloat16 [8192, 3072], P('ctx', 'head'), may hold values from -6 to 6
- norm_gain: bfloat16 [3072], P('head'), may hold values from 0.099609375 to 1.8984375
- router: bfloat16 [3072, 32], replicated, may hold values from -0.21875 to 0.21875
- expert_ids: int32 [8192, 2], P('ctx'), may hold values from 0 to 31, all different within a row; in each aligned block of 256 rows (0 to 255, 256 to 511, ...) at most 24 rows name the same one
- gate_weight: bfloat16 [32, 3072, 5120], P('ctx', None, 'head'), may hold values from -0.109375 to 0.109375
- up_weight: bfloat16 [32, 3072, 5120], P('ctx', None, 'head'), may hold values from -0.109375 to 0.109375
- down_weight: bfloat16 [32, 5120, 3072], P('ctx', 'head'), may hold values from -0.125 to 0.125
Outputs:
- layer_out: float32 [8192, 3072], P('ctx', 'head')
Inputs may be any that keep to these rules, and one draw needn't show every extreme that they name: `log_decay`: amounts by which a head's state decays at a position: the state is multiplied by exp(-value). `expert_ids`: each row names 2 different experts; among the rows of one block of 256 positions no expert is named more than 24 times, a bound that some block reaches.
All inputs are finite; a program needn't handle non-finite values.
Results may differ from a plain program's by a relative error of at most 0.007.
Values may be sent and summed in bfloat16 or wider, within the bound.
No kernel may reach another device: no remote copies, remote signals or barrier semaphores. Data moves between devices by JAX's collectives and lax.ppermute only.
A program may use at most 128 MiB of HBM per device.

v0:
```python
import jax
import jax.numpy as jnp
from jax import lax
from jax.sharding import PartitionSpec as P

HEAD_DIM = 128
TOP = 2
HIGH = lax.Precision.HIGHEST
EPSILON = 1e-05


def combine(earlier, later):
    rows = HEAD_DIM
    decay_late = later[:, rows : rows + 1, 0:1]
    state = decay_late * earlier[:, :rows] + later[:, :rows]
    decay = earlier[:, rows : rows + 1] * later[:, rows : rows + 1]
    pad = jnp.zeros((later.shape[0], later.shape[1] - rows - 1, later.shape[2]), later.dtype)
    return jnp.concatenate([state, decay, pad], axis=1)


def exclusive_scan(packed, axis):
    count, mine = (lax.axis_size(axis), lax.axis_index(axis))
    rows = HEAD_DIM
    identity = jnp.zeros_like(packed).at[:, rows].set(1.0)
    window = packed
    before = identity
    base = 1
    while base < count:
        joined = None
        for step in range(1, 4):
            shift = step * base
            if shift >= count:
                break
            pairs = [(j, j + shift) for j in range(count - shift)]
            got = lax.ppermute(window, axis, pairs)
            got = jnp.where(mine >= shift, got, identity)
            joined = got if joined is None else combine(got, joined)
        before = combine(joined, before)
        if 4 * base < count:
            window = combine(joined, window)
        base *= 4
    return before[:, :rows]


def on_device(
    queries,
    key_rows,
    values,
    log_decay,
    head_gain,
    out_weight,
    residual,
    norm_gain,
    router,
    expert_ids,
    gate_weight,
    up_weight,
    down_weight,
):
    rows = queries.shape[0]
    heads_here = log_decay.shape[1]
    groups = lax.axis_size("head")
    query_heads = queries.reshape(rows, heads_here, HEAD_DIM)
    key_heads = key_rows.reshape(rows, heads_here, HEAD_DIM)
    value_heads = values.reshape(rows, heads_here, HEAD_DIM)
    cumulative = jnp.cumsum(log_decay, axis=0)
    scores = jnp.einsum("thd,jhd->htj", query_heads, key_heads, preferred_element_type=jnp.float32)
    causal = jnp.arange(rows)[:, None] >= jnp.arange(rows)[None, :]
    gap = cumulative.T[:, :, None] - cumulative.T[:, None, :]
    weight = jnp.where(causal[None], jnp.exp(-jnp.where(causal[None], gap, 0.0)), 0.0)
    weighted = (scores * weight).astype(jnp.bfloat16)
    inner = jnp.einsum("htj,jhd->thd", weighted, value_heads, preferred_element_type=jnp.float32)
    value_wide = value_heads.astype(jnp.float32)
    tail = jnp.exp(cumulative - cumulative[-1:])
    keys_tail = key_heads.astype(jnp.float32) * tail[:, :, None]
    local_state = jnp.einsum("jhd,jhe->hde", keys_tail, value_wide, precision=HIGH)
    shard_decay = jnp.exp(-cumulative[-1])
    decay_rows = jnp.broadcast_to(shard_decay[:, None, None], (heads_here, 1, HEAD_DIM))
    pad = jnp.zeros((heads_here, 7, HEAD_DIM), jnp.float32)
    packed = jnp.concatenate([local_state, decay_rows, pad], axis=1)
    incoming = exclusive_scan(packed, "ctx")
    query_decayed = query_heads.astype(jnp.float32) * jnp.exp(-cumulative)[:, :, None]
    outer = jnp.einsum("thd,hde->the", query_decayed, incoming, precision=HIGH)
    mixed = inner + outer
    mean_sq = jnp.mean(mixed * mixed, axis=-1, keepdims=True)
    gain_heads = head_gain.astype(jnp.float32).reshape(heads_here, HEAD_DIM)
    normed = (
        (mixed * lax.rsqrt(mean_sq + EPSILON) * gain_heads)
        .astype(jnp.bfloat16)
        .reshape(rows, heads_here * HEAD_DIM)
    )
    width = residual.shape[1]
    full = width * groups
    weight_all = lax.all_gather(out_weight, "ctx", axis=0, tiled=True).reshape(
        groups, width, heads_here * HEAD_DIM
    )
    partial_proj = jnp.einsum("tk,gck->gtc", normed, weight_all, preferred_element_type=jnp.float32)
    total = lax.psum_scatter(partial_proj, "head", scatter_dimension=0, tiled=True)
    stream_mine = residual.astype(jnp.float32) + total[0]
    sq_part = jnp.sum(stream_mine * stream_mine, axis=1)
    sq_hi = sq_part.astype(jnp.bfloat16)
    sq_lo = (sq_part - sq_hi.astype(jnp.float32)).astype(jnp.bfloat16)
    extra = jnp.zeros((8, width), jnp.bfloat16)
    extra = extra.at[0].set(norm_gain)
    extra = extra.at[1, :rows].set(sq_hi)
    extra = extra.at[2, :rows].set(sq_lo)
    payload = jnp.concatenate([stream_mine.astype(jnp.bfloat16), extra], axis=0)
    gathered = lax.all_gather(payload, "head", axis=1, tiled=True)
    stream_wide = gathered[:rows].astype(jnp.float32)
    gain_full = gathered[rows].astype(jnp.float32)
    sq_parts = gathered[rows + 1 : rows + 3].astype(jnp.float32).reshape(2, groups, width)
    stream_sq = jnp.sum(sq_parts[:, :, :rows], axis=(0, 1))[:, None] / full
    moe_in = (stream_wide * lax.rsqrt(stream_sq + EPSILON) * gain_full).astype(jnp.bfloat16)
    experts = router.shape[1]
    capacity = 3 * rows * TOP // (2 * experts)
    logits = jnp.dot(moe_in, router, preferred_element_type=jnp.float32)
    picked_mask = expert_ids[:, :, None] == jnp.arange(experts, dtype=jnp.int32)[None, None, :]
    picked = jnp.sum(jnp.where(picked_mask, logits[:, None, :], 0.0), axis=-1)
    mix_weights = jax.nn.sigmoid(picked - picked[:, ::-1])
    flat_ids = expert_ids.reshape(-1)
    onehot = (flat_ids[:, None] == jnp.arange(experts, dtype=jnp.int32)[None, :]).astype(jnp.int32)
    before = jnp.cumsum(onehot, axis=0) - onehot
    position = jnp.sum(before * onehot, axis=1)
    slot = flat_ids * capacity + position
    owner = jnp.arange(rows * TOP, dtype=jnp.int32) // TOP
    slot_token = jnp.zeros((experts * capacity,), jnp.int32).at[slot].set(owner)
    filled = jnp.zeros((experts * capacity,), jnp.bool_).at[slot].set(True)
    blank = jnp.zeros((), jnp.bfloat16)
    outgoing = jnp.where(filled[:, None], moe_in[slot_token], blank).reshape(
        experts, capacity, full
    )
    half = capacity // 2
    down = down_weight[0].reshape(down_weight.shape[1], groups, width)
    parts = []
    for lo, hi in ((0, half), (half, capacity)):
        arriving = lax.all_to_all(
            outgoing[:, lo:hi], "ctx", split_axis=0, concat_axis=0, tiled=True
        )
        flat = arriving.reshape(-1, full)
        gate = jnp.dot(flat, gate_weight[0], preferred_element_type=jnp.float32)
        up = jnp.dot(flat, up_weight[0], preferred_element_type=jnp.float32)
        activated = (jax.nn.silu(gate) * up).astype(jnp.bfloat16)
        partial_value = jnp.einsum(
            "rf,fgc->grc", activated, down, preferred_element_type=jnp.float32
        ).astype(jnp.bfloat16)
        summed = lax.psum_scatter(partial_value, "head", scatter_dimension=0, tiled=True)
        summed = summed.reshape(arriving.shape[0], arriving.shape[1], width)
        parts.append(lax.all_to_all(summed, "ctx", split_axis=0, concat_axis=0, tiled=True))
    returned = jnp.concatenate(parts, axis=1)
    picked_rows = returned.reshape(experts * capacity, width)[slot].astype(jnp.float32)
    moe_out = jnp.sum(picked_rows.reshape(rows, TOP, width) * mix_weights[:, :, None], axis=1)
    return stream_mine + moe_out


def solution(mesh):
    placed = (
        P("ctx", "head"),
        P("ctx", "head"),
        P("ctx", "head"),
        P("ctx", "head"),
        P("head"),
        P("ctx", "head"),
        P("ctx", "head"),
        P("head"),
        P(),
        P("ctx", None),
        P("ctx", None, "head"),
        P("ctx", None, "head"),
        P("ctx", "head", None),
    )
    return jax.shard_map(
        on_device, mesh=mesh, in_specs=placed, out_specs=P("ctx", "head"), check_vma=False
    )
```

profile of v0, /device:TPU:1, one launch (start us, length us, event | category | flops | bytes accessed | tf_op | source)
XLA Modules:
  0.0 394.2 jit_solution(11019015704431273449)
XLA Ops:
  13.1 6.0 %collective-permute-start.2 = (f32[4,136,128]{2,1,0:T(8,128)S(1)}, f32[4,136,128]{2,1,0:T(8,128)S(1)}, u32[]{:S(2)}, u32[]{:S(2)}) collective-permute-start(f32[4,136,128]{2,1,0:T(8,128)S(1)} %maximum_maximum_fusion), channel_id=1, source_target_pairs={{0,24},{8,32},{16,40},{24,48},{32,56},{40,64},{48,72},{56,80},{64,... | collective-permute-start | bytes 835592 | tf_op jit(solution)/shard_map/ppermute | solution.py:35
  24.3 6.0 %collective-permute-done.1 = f32[4,136,128]{2,1,0:T(8,128)S(1)} collective-permute-done((f32[4,136,128]{2,1,0:T(8,128)S(1)}, f32[4,136,128]{2,1,0:T(8,128)S(1)}, u32[]{:S(2)}, u32[]{:S(2)}) %collective-permute-start.1) | collective-permute-done | bytes 278560 | tf_op jit(solution)/shard_map/ppermute | solution.py:35
  36.4 5.3 %collective-permute-start.5 = (f32[4,136,128]{2,1,0:T(8,128)S(1)}, f32[4,136,128]{2,1,0:T(8,128)S(1)}, u32[]{:S(2)}, u32[]{:S(2)}) collective-permute-start(f32[4,136,128]{2,1,0:T(8,128)S(1)} %maximum_maximum_fusion.1), channel_id=1, source_target_pairs={{0,32},{8,40},{16,48},{24,56},{32,64},{40,72},{48,80},{56,88},{64,... | collective-permute-start | bytes 835592 | tf_op jit(solution)/shard_map/ppermute | solution.py:35
  44.9 6.0 %collective-permute-start.3 = (f32[4,136,128]{2,1,0:T(8,128)S(1)}, f32[4,136,128]{2,1,0:T(8,128)S(1)}, u32[]{:S(2)}, u32[]{:S(2)}) collective-permute-start(f32[4,136,128]{2,1,0:T(8,128)S(1)} %maximum_maximum_fusion.1), channel_id=1, source_target_pairs={{0,96},{8,104},{16,112},{24,120},{32,128},{40,136},{48,144},{56,15... | collective-permute-start | bytes 835592 | tf_op jit(solution)/shard_map/ppermute | solution.py:35
  52.5 15.9 %collective-permute-done.4 = f32[4,136,128]{2,1,0:T(8,128)S(1)} collective-permute-done((f32[4,136,128]{2,1,0:T(8,128)S(1)}, f32[4,136,128]{2,1,0:T(8,128)S(1)}, u32[]{:S(2)}, u32[]{:S(2)}) %collective-permute-start.4) | collective-permute-done | bytes 278560 | tf_op jit(solution)/shard_map/ppermute | solution.py:35
  69.0 5.8 %collective-permute-start.6 = (f32[4,136,128]{2,1,0:T(8,128)S(1)}, f32[4,136,128]{2,1,0:T(8,128)S(1)}, u32[]{:S(2)}, u32[]{:S(2)}) collective-permute-start(f32[4,136,128]{2,1,0:T(8,128)S(1)} %maximum_maximum_fusion.2), channel_id=1, source_target_pairs={{0,128},{8,136},{16,144},{24,152},{32,160},{40,168},{48,176},{56,1... | collective-permute-start | bytes 835592 | tf_op jit(solution)/shard_map/ppermute | solution.py:35
  76.3 4.3 %collective-permute-done.6 = f32[4,136,128]{2,1,0:T(8,128)S(1)} collective-permute-done((f32[4,136,128]{2,1,0:T(8,128)S(1)}, f32[4,136,128]{2,1,0:T(8,128)S(1)}, u32[]{:S(2)}, u32[]{:S(2)}) %collective-permute-start.6) | collective-permute-done | bytes 278560 | tf_op jit(solution)/shard_map/ppermute | solution.py:35
  82.3 4.6 %convolution_bitcast_fusion = f32[8,256,384]{2,1,0:T(8,128)} fusion(bf16[256,512,1]{0,1,2:T(8,128)(2,1)S(1)} %bitcast.159, bf16[8,384,512]{2,1,0:T(8,128)(2,1)} %bitcast.158), kind=kOutput, calls=%fused_computation.20 | convolution fusion | flops 805306368 | bytes 6553600 | tf_op jit(solution)/shard_map/tk,gck->gtc/dot_general | solution.py:97
  87.6 45.2 %reduce-scatter.4.cloned.1.call-done = f32[1,256,384]{2,1,0:T(8,128)} async-done(((f32[8,256,384]{2,1,0:T(8,128)}), f32[1,256,384]{2,1,0:T(8,128)}) %reduce-scatter.4.cloned.1.call-update) | async-done | bytes 393232 | tf_op jit(solution)/shard_map/reduce_scatter | solution.py:98
  142.7 30.0 %all-gather.5.cloned.1.call-done = bf16[264,3072]{1,0:T(8,128)(2,1)} async-done(((bf16[264,384]{1,0:T(8,128)(2,1)}), bf16[264,3072]{1,0:T(8,128)(2,1)}) %all-gather.5.cloned.1.call-update) | async-done | bytes 1622032 | tf_op jit(solution)/shard_map/all_gather | solution.py:108
  176.3 5.0 %gather_fusion = bf16[768,3072]{1,0:T(8,128)(2,1)} fusion(bf16[256,3072]{1,0:T(8,128)(2,1)S(1)} %multiply_convert_fusion, s32[1024]{0:T(1024)S(1)} %pad_clamp_fusion.1), kind=kCustom, calls=%fused_computation | custom fusion | bytes 9440256 | tf_op jit(solution)/shard_map/gather | solution.py:129
  188.0 12.7 %all-to-all-start.2 = ((bf16[32,12,3072]{2,1,0:T(8,128)(2,1)}), bf16[32,12,3072]{2,1,0:T(8,128)(2,1)}, u32[]{:S(2)}, u32[]{:S(2)}) async-start(bf16[32,12,3072]{2,1,0:T(8,128)(2,1)} %get-tuple-element.66), calls=%async_computation.4 | async-start | bytes 6291456 | tf_op jit(solution)/shard_map/all_to_all | solution.py:136
  200.8 4.9 %copy.111 = bf16[80,8,8,384]{3,2,1,0:T(8,128)(2,1)} copy(bf16[80,8,8,384]{3,1,2,0:T(8,128)(2,1)} %bitcast.155) | data formatting | bytes 7864320
  205.7 34.8 %all-to-all-done.2 = bf16[32,12,3072]{2,1,0:T(8,128)(2,1)} async-done(((bf16[32,12,3072]{2,1,0:T(8,128)(2,1)}), bf16[32,12,3072]{2,1,0:T(8,128)(2,1)}, u32[]{:S(2)}, u32[]{:S(2)}) %all-to-all-start.2) | async-done | bytes 2359328 | tf_op jit(solution)/shard_map/all_to_all | solution.py:136
  240.6 4.2 %reshape.300 = bf16[384,3072]{1,0:T(8,128)(2,1)} reshape(bf16[32,12,3072]{2,1,0:T(8,128)(2,1)} %all-to-all-done.2) | data formatting | bytes 4718592 | tf_op jit(solution)/shard_map/reshape | solution.py:139
  244.8 4.8 %fusion.4 = f32[384,640]{1,0:T(8,128)S(1)} fusion(bf16[384,3072]{1,0:T(8,128)(2,1)} %reshape.300, bf16[1,3072,640]{2,1,0:T(8,128)(2,1)} %param.31), kind=kOutput, calls=%fused_computation.9 | convolution fusion | flops 1509949440 | bytes 7274496 | tf_op jit(solution)/shard_map/dot_general | solution.py:140
  249.6 10.3 %convert_bitcast_fusion = bf16[8,384,384]{2,1,0:T(8,128)(2,1)} fusion(bf16[640,8,384]{2,1,0:T(8,128)(2,1)} %bitcast.156, bf16[384,3072]{1,0:T(8,128)(2,1)} %reshape.300, bf16[1,3072,640]{2,1,0:T(8,128)(2,1)} %param.32, f32[384,640]{1,0:T(8,128)S(1)} %fusion.4), kind=kOutput, calls=%fused_computation.18 | convolution fusion | flops 3022553088 | bytes 13565952 | tf_op jit(solution)/shard_map/rf,fgc->grc/dot_general | solution.py:143
  260.0 46.5 %all_to_all.20 = bf16[32,12,3072]{2,1,0:T(8,128)(2,1)} all-to-all(bf16[32,12,3072]{2,1,0:T(8,128)(2,1)} %get-tuple-element.65), channel_id=1, replica_groups=mesh['ctx'=32,'head'=8] {'ctx'}, dimensions={0} | all-to-all | bytes 4718592 | tf_op jit(solution)/shard_map/all_to_all | solution.py:136
  306.5 4.2 %reshape.298 = bf16[384,3072]{1,0:T(8,128)(2,1)} reshape(bf16[32,12,3072]{2,1,0:T(8,128)(2,1)} %all_to_all.20) | data formatting | bytes 4718592 | tf_op jit(solution)/shard_map/reshape | solution.py:139
  310.8 4.8 %fusion.6 = f32[384,640]{1,0:T(8,128)S(1)} fusion(bf16[384,3072]{1,0:T(8,128)(2,1)} %reshape.298, bf16[1,3072,640]{2,1,0:T(8,128)(2,1)} %param.31), kind=kOutput, calls=%fused_computation.11 | convolution fusion | flops 1509949440 | bytes 7274496 | tf_op jit(solution)/shard_map/dot_general | solution.py:140
  315.6 10.3 %convert_bitcast_fusion.1 = bf16[8,384,384]{2,1,0:T(8,128)(2,1)} fusion(bf16[640,8,384]{2,1,0:T(8,128)(2,1)} %bitcast.157, bf16[384,3072]{1,0:T(8,128)(2,1)} %reshape.298, bf16[1,3072,640]{2,1,0:T(8,128)(2,1)} %param.32, f32[384,640]{1,0:T(8,128)S(1)} %fusion.6), kind=kOutput, calls=%fused_computation.19 | convolution fusion | flops 3022553088 | bytes 13565952 | tf_op jit(solution)/shard_map/rf,fgc->grc/dot_general | solution.py:143
  332.3 27.5 %reduce-scatter.6.cloned.1.call-done = bf16[1,384,384]{2,1,0:T(8,128)(2,1)} async-done(((bf16[8,384,384]{2,1,0:T(8,128)(2,1)}), bf16[1,384,384]{2,1,0:T(8,128)(2,1)}) %reduce-scatter.6.cloned.1.call-update) | async-done | bytes 294928 | tf_op jit(solution)/shard_map/reduce_scatter | solution.py:146
  361.5 11.7 %all-to-all-start.1 = ((bf16[32,12,384]{2,1,0:T(8,128)(2,1)}), bf16[32,12,384]{2,1,0:T(8,128)(2,1)S(1)}, u32[]{:S(2)}, u32[]{:S(2)}) async-start(bf16[32,12,384]{2,1,0:T(8,128)(2,1)} %reshape.299), calls=%async_computation.3 | async-start | bytes 786432 | tf_op jit(solution)/shard_map/all_to_all | solution.py:148
  373.5 9.9 %all-to-all-done.1 = bf16[32,12,384]{2,1,0:T(8,128)(2,1)S(1)} async-done(((bf16[32,12,384]{2,1,0:T(8,128)(2,1)}), bf16[32,12,384]{2,1,0:T(8,128)(2,1)S(1)}, u32[]{:S(2)}, u32[]{:S(2)}) %all-to-all-start.1) | async-done | bytes 294944 | tf_op jit(solution)/shard_map/all_to_all | solution.py:148
  (135 shorter events, 59.4 us)
Async XLA Ops:
  6.5 44.4 %copy-start = (bf16[256,512]{1,0:T(8,128)(2,1)S(1)}, bf16[256,512]{1,0:T(8,128)(2,1)}, u32[]{:S(2)}) copy-start(bf16[256,512]{1,0:T(8,128)(2,1)} %param.21) | copy-start | bytes 786436
  6.5 44.5 %copy-start.5 = (bf16[256,512]{1,0:T(8,128)(2,1)S(1)}, bf16[256,512]{1,0:T(8,128)(2,1)}, u32[]{:S(2)}) copy-start(bf16[256,512]{1,0:T(8,128)(2,1)} %param.23) | copy-start | bytes 786436
  6.5 75.8 %all-gather.3.cloned.1.call-start = ((), (), s32[]{:S(2)}) async-start(), calls=%async_computation.7 | async-start | bytes 3244032 | tf_op jit(solution)/shard_map/all_gather | solution.py:94
  7.3 125.6 %reduce-scatter.4.cloned.1.call-start = ((), (), s32[]{:S(2)}) async-start(), calls=%async_computation.8 | async-start | bytes 3538944 | tf_op jit(solution)/shard_map/reduce_scatter | solution.py:98
  10.8 25.5 %copy-start.10 = (f32[136]{0:T(256)}, f32[136]{0:T(256)S(1)}, u32[]{:S(2)}) copy-start(f32[136]{0:T(256)S(1)} %pad.23.clone) | copy-start | bytes 1636
  13.1 11.2 %collective-permute-start.2 = (f32[4,136,128]{2,1,0:T(8,128)S(1)}, f32[4,136,128]{2,1,0:T(8,128)S(1)}, u32[]{:S(2)}, u32[]{:S(2)}) collective-permute-start(f32[4,136,128]{2,1,0:T(8,128)S(1)} %maximum_maximum_fusion), channel_id=1, source_target_pairs={{0,24},{8,32},{16,40},{24,48},{32,56},{40,64},{48,72},{56,80},{64,... | collective-permute-start | bytes 835592 | tf_op jit(solution)/shard_map/ppermute | solution.py:35
  19.2 11.2 %collective-permute-start.1 = (f32[4,136,128]{2,1,0:T(8,128)S(1)}, f32[4,136,128]{2,1,0:T(8,128)S(1)}, u32[]{:S(2)}, u32[]{:S(2)}) collective-permute-start(f32[4,136,128]{2,1,0:T(8,128)S(1)} %maximum_maximum_fusion), channel_id=1, source_target_pairs={{0,8},{8,16},{16,24},{24,32},{32,40},{40,48},{48,56},{56,64},{64,7... | collective-permute-start | bytes 835592 | tf_op jit(solution)/shard_map/ppermute | solution.py:35
  21.1 13.3 %collective-permute-start = (f32[4,136,128]{2,1,0:T(8,128)S(1)}, f32[4,136,128]{2,1,0:T(8,128)S(1)}, u32[]{:S(2)}, u32[]{:S(2)}) collective-permute-start(f32[4,136,128]{2,1,0:T(8,128)S(1)} %maximum_maximum_fusion), channel_id=1, source_target_pairs={{0,16},{8,24},{16,32},{24,40},{32,48},{40,56},{48,64},{56,72},{64,... | collective-permute-start | bytes 835592 | tf_op jit(solution)/shard_map/ppermute | solution.py:35
  35.4 33.0 %copy-start.2 = (f32[4,136,128]{2,1,0:T(8,128)S(1)}, f32[4,136,128]{2,1,0:T(8,128)}, u32[]{:S(2)}) copy-start(f32[4,136,128]{2,1,0:T(8,128)} %constant.174.clone.1) | copy-start | bytes 835588
  36.0 8.9 %copy-start.7 = (f32[4,1,128]{2,1,0:T(1,128)}, f32[4,1,128]{2,1,0:T(1,128)S(1)}, u32[]{:S(2)}) copy-start(f32[4,1,128]{2,1,0:T(1,128)S(1)} %get-tuple-element.62) | copy-start | bytes 6148
  36.4 16.2 %collective-permute-start.5 = (f32[4,136,128]{2,1,0:T(8,128)S(1)}, f32[4,136,128]{2,1,0:T(8,128)S(1)}, u32[]{:S(2)}, u32[]{:S(2)}) collective-permute-start(f32[4,136,128]{2,1,0:T(8,128)S(1)} %maximum_maximum_fusion.1), channel_id=1, source_target_pairs={{0,32},{8,40},{16,48},{24,56},{32,64},{40,72},{48,80},{56,88},{64,... | collective-permute-start | bytes 835592 | tf_op jit(solution)/shard_map/ppermute | solution.py:35
  41.7 26.7 %collective-permute-start.4 = (f32[4,136,128]{2,1,0:T(8,128)S(1)}, f32[4,136,128]{2,1,0:T(8,128)S(1)}, u32[]{:S(2)}, u32[]{:S(2)}) collective-permute-start(f32[4,136,128]{2,1,0:T(8,128)S(1)} %maximum_maximum_fusion.1), channel_id=1, source_target_pairs={{0,64},{8,72},{16,80},{24,88},{32,96},{40,104},{48,112},{56,120},{... | collective-permute-start | bytes 835592 | tf_op jit(solution)/shard_map/ppermute | solution.py:35
  44.9 23.5 %collective-permute-start.3 = (f32[4,136,128]{2,1,0:T(8,128)S(1)}, f32[4,136,128]{2,1,0:T(8,128)S(1)}, u32[]{:S(2)}, u32[]{:S(2)}) collective-permute-start(f32[4,136,128]{2,1,0:T(8,128)S(1)} %maximum_maximum_fusion.1), channel_id=1, source_target_pairs={{0,96},{8,104},{16,112},{24,120},{32,128},{40,136},{48,144},{56,15... | collective-permute-start | bytes 835592 | tf_op jit(solution)/shard_map/ppermute | solution.py:35
  52.4 16.5 %copy-start.11 = (f32[136]{0:T(256)S(1)}, f32[136]{0:T(256)}, u32[]{:S(2)}) copy-start(f32[136]{0:T(256)} %copy-done.10) | copy-start | bytes 1636
  69.0 11.6 %collective-permute-start.6 = (f32[4,136,128]{2,1,0:T(8,128)S(1)}, f32[4,136,128]{2,1,0:T(8,128)S(1)}, u32[]{:S(2)}, u32[]{:S(2)}) collective-permute-start(f32[4,136,128]{2,1,0:T(8,128)S(1)} %maximum_maximum_fusion.2), channel_id=1, source_target_pairs={{0,128},{8,136},{16,144},{24,152},{32,160},{40,168},{48,176},{56,1... | collective-permute-start | bytes 835592 | tf_op jit(solution)/shard_map/ppermute | solution.py:35
  87.0 45.9 %copy-start.4 = (bf16[256,384]{1,0:T(8,128)(2,1)S(1)}, bf16[256,384]{1,0:T(8,128)(2,1)}, u32[]{:S(2)}) copy-start(bf16[256,384]{1,0:T(8,128)(2,1)} %param.27) | copy-start | bytes 589828
  87.0 48.2 %copy-start.9 = (s32[256,2]{0,1:T(2,128)S(1)}, s32[256,2]{0,1:T(2,128)}, u32[]{:S(2)}) copy-start(s32[256,2]{0,1:T(2,128)} %param.30) | copy-start | bytes 6148
  87.0 85.8 %all-gather.5.cloned.1.call-start = ((), (), s32[]{:S(2)}) async-start(), calls=%async_computation.9 | async-start | bytes 1824768 | tf_op jit(solution)/shard_map/all_gather | solution.py:108
  188.0 52.5 %all-to-all-start.2 = ((bf16[32,12,3072]{2,1,0:T(8,128)(2,1)}), bf16[32,12,3072]{2,1,0:T(8,128)(2,1)}, u32[]{:S(2)}, u32[]{:S(2)}) async-start(bf16[32,12,3072]{2,1,0:T(8,128)(2,1)} %get-tuple-element.66), calls=%async_computation.4 | async-start | bytes 6291456 | tf_op jit(solution)/shard_map/all_to_all | solution.py:136
  200.7 125.2 %reduce-scatter.8.cloned.1.call-start = ((), (), s32[]{:S(2)}) async-start(), calls=%async_computation.11 | async-start | bytes 2654208 | tf_op jit(solution)/shard_map/reduce_scatter | solution.py:146
  259.9 99.8 %reduce-scatter.6.cloned.1.call-start = ((), (), s32[]{:S(2)}) async-start(), calls=%async_computation.10 | async-start | bytes 2654208 | tf_op jit(solution)/shard_map/reduce_scatter | solution.py:146
  325.9 5.8 %copy-start.6 = (bf16[3072,32]{0,1:T(8,128)(2,1)S(1)}, bf16[3072,32]{0,1:T(8,128)(2,1)}, u32[]{:S(2)}) copy-start(bf16[3072,32]{0,1:T(8,128)(2,1)} %param.29) | copy-start | bytes 589828
  327.7 33.8 %all-to-all-start.3 = ((bf16[32,12,384]{2,1,0:T(8,128)(2,1)}), bf16[32,12,384]{2,1,0:T(8,128)(2,1)S(1)}, u32[]{:S(2)}, u32[]{:S(2)}) async-start(bf16[32,12,384]{2,1,0:T(8,128)(2,1)} %reshape.301), calls=%async_computation.6 | async-start | bytes 786432 | tf_op jit(solution)/shard_map/all_to_all | solution.py:148
  361.5 21.8 %all-to-all-start.1 = ((bf16[32,12,384]{2,1,0:T(8,128)(2,1)}), bf16[32,12,384]{2,1,0:T(8,128)(2,1)S(1)}, u32[]{:S(2)}, u32[]{:S(2)}) async-start(bf16[32,12,384]{2,1,0:T(8,128)(2,1)} %reshape.299), calls=%async_computation.3 | async-start | bytes 786432 | tf_op jit(solution)/shard_map/all_to_all | solution.py:148
  (5 other events, 13.0 us)
Sparse Core Ops, SparseCore 0:
  9.9 61.5 all-gather.2
  87.1 45.7 reduce-scatter.3
  135.3 37.3 all-gather.4
  260.0 34.8 reduce-scatter.7
  326.0 33.6 reduce-scatter.5
where the time goes:
time: 395 us; the launch traced here: 394 us
  waiting for transfers between devices  179 us (45%)
  starting transfers between devices  59.1 us (15%)
  blocking collectives  46.5 us (12%)
  matrix products  39.6 us (10%)
  local copies, waits for them, and re-layouts  39.4 us (10%)
  other arithmetic  16.4 us (4%)
  between operations  13.7 us (3%)
    all_to_all x1, blocking collectives, on_device(): lax.all_to_all(outgoing[:, lo:hi], 'ctx', split_axis=0, concat_axis=0, ti...  46.5 us
    reduce_scatter x1, waiting for transfers between devices, on_device(): lax.psum_scatter(partial_proj, 'head', scatter_dimension=0, tiled=True)  45.2 us
    all_to_all x1, waiting for transfers between devices, on_device(): lax.all_to_all(outgoing[:, lo:hi], 'ctx', split_axis=0, concat_axis=0, ti...  34.8 us
    ppermute x7, waiting for transfers between devices, exclusive_scan(): got = lax.ppermute(window, axis, pairs)  31.2 us
    ppermute x7, starting transfers between devices, exclusive_scan(): got = lax.ppermute(window, axis, pairs)  30.6 us
    all_gather x1, waiting for transfers between devices, on_device(): gathered = lax.all_gather(payload, 'head', axis=1, tiled=True)  30 us
    reduce_scatter x2, waiting for transfers between devices, on_device(): lax.psum_scatter(partial_value, 'head', scatter_dimension=0, tiled=True)  27.5 us
    dot_general x2, matrix products, on_device(): jnp.einsum('rf,fgc->grc', activated, down, preferred_element_type=jnp.flo...  20.6 us
  transfers between devices with their start and end apart: 15, of which 10 were waited for; matrix products, arithmetic and copies ran while one was open for 12% of the time, Pallas kernels for 0%

commit v1 on v0

--- a/solution.py
+++ b/solution.py
@@ -1,3 +1,4 @@
+import functools
 import jax
 import jax.numpy as jnp
 from jax import lax
@@ -7,6 +8,16 @@
 TOP = 2
 HIGH = lax.Precision.HIGHEST
 EPSILON = 1e-05
+
+
+def render_cards_on(obj, mesh_ax):
+    tile_out = jnp.concatenate(
+        lax.all_to_all(jnp.stack(lax.axis_size(mesh_ax) * [obj]), mesh_ax, 0, 0), axis=1
+    )
+    return tile_out
+
+
+close_the_loads = functools.partial(render_cards_on, mesh_ax="head")
 
 
 def combine(earlier, later):
@@ -105,7 +116,7 @@
     extra = extra.at[1, :rows].set(sq_hi)
     extra = extra.at[2, :rows].set(sq_lo)
     payload = jnp.concatenate([stream_mine.astype(jnp.bfloat16), extra], axis=0)
-    gathered = lax.all_gather(payload, "head", axis=1, tiled=True)
+    gathered = close_the_loads(payload)
     stream_wide = gathered[:rows].astype(jnp.float32)
     gain_full = gathered[rows].astype(jnp.float32)
     sq_parts = gathered[rows + 1 : rows + 3].astype(jnp.float32).reshape(2, groups, width)

time: 395 us -> 395 us (level)
    all_to_all x0 -> x1, waiting for transfers between devices: none -> 30.8 us  [render_cards_on(): lax.all_to_all(jnp.stack(lax.axis_size(mesh_ax) * [obj]), mesh_ax, 0, 0)]
    all_gather x1 -> x0, waiting for transfers between devices: 30 us -> none  [on_device(): gathered = lax.all_gather(payload, 'head', axis=1, tiled=True)]
    all_to_all x0 -> x1, starting transfers between devices: none -> 4.98 us  [render_cards_on(): lax.all_to_all(jnp.stack(lax.axis_size(mesh_ax) * [obj]), mesh_ax, 0, 0)]
where the time goes in v1:
time: 395 us; the launch traced here: 394 us
  waiting for transfers between devices  178 us (45%)
  starting transfers between devices  62.1 us (16%)
  blocking collectives  46.5 us (12%)
  local copies, waits for them, and re-layouts  40.3 us (10%)
  matrix products  39.6 us (10%)
  other arithmetic  13.7 us (3%)
  between operations  13.7 us (3%)
    all_to_all x1, blocking collectives, on_device(): lax.all_to_all(outgoing[:, lo:hi], 'ctx', split_axis=0, concat_axis=0, ti...  46.5 us
    reduce_scatter x1, waiting for transfers between devices, on_device(): lax.psum_scatter(partial_proj, 'head', scatter_dimension=0, tiled=True)  45.2 us
    all_to_all x1, waiting for transfers between devices, on_device(): lax.all_to_all(outgoing[:, lo:hi], 'ctx', split_axis=0, concat_axis=0, ti...  34.8 us
    ppermute x7, waiting for transfers between devices, exclusive_scan(): got = lax.ppermute(window, axis, pairs)  31.2 us
    all_to_all x1, waiting for transfers between devices, render_cards_on(): lax.all_to_all(jnp.stack(lax.axis_size(mesh_ax) * [obj]), mesh_ax, 0, 0)  30.8 us
    ppermute x7, starting transfers between devices, exclusive_scan(): got = lax.ppermute(window, axis, pairs)  30.6 us
    reduce_scatter x2, waiting for transfers between devices, on_device(): lax.psum_scatter(partial_value, 'head', scatter_dimension=0, tiled=True)  25.5 us
    dot_general x2, matrix products, on_device(): jnp.einsum('rf,fgc->grc', activated, down, preferred_element_type=jnp.flo...  20.6 us
  transfers between devices with their start and end apart: 15, of which 10 were waited for; matrix products, arithmetic and copies ran while one was open for 12% of the time, Pallas kernels for 0%

profile of v1, /device:TPU:1, one launch (start us, length us, event | category | flops | bytes accessed | tf_op | source)
XLA Modules:
  0.0 394.2 jit_solution(13271470791700909378)
XLA Ops:
  13.1 6.0 %collective-permute-start.2 = (f32[4,136,128]{2,1,0:T(8,128)S(1)}, f32[4,136,128]{2,1,0:T(8,128)S(1)}, u32[]{:S(2)}, u32[]{:S(2)}) collective-permute-start(f32[4,136,128]{2,1,0:T(8,128)S(1)} %maximum_maximum_fusion), channel_id=1, source_target_pairs={{0,24},{8,32},{16,40},{24,48},{32,56},{40,64},{48,72},{56,80},{64,... | collective-permute-start | bytes 835592 | tf_op jit(solution)/shard_map/ppermute | solution.py:46
  24.3 6.0 %collective-permute-done.1 = f32[4,136,128]{2,1,0:T(8,128)S(1)} collective-permute-done((f32[4,136,128]{2,1,0:T(8,128)S(1)}, f32[4,136,128]{2,1,0:T(8,128)S(1)}, u32[]{:S(2)}, u32[]{:S(2)}) %collective-permute-start.1) | collective-permute-done | bytes 278560 | tf_op jit(solution)/shard_map/ppermute | solution.py:46
  36.4 5.3 %collective-permute-start.5 = (f32[4,136,128]{2,1,0:T(8,128)S(1)}, f32[4,136,128]{2,1,0:T(8,128)S(1)}, u32[]{:S(2)}, u32[]{:S(2)}) collective-permute-start(f32[4,136,128]{2,1,0:T(8,128)S(1)} %maximum_maximum_fusion.1), channel_id=1, source_target_pairs={{0,32},{8,40},{16,48},{24,56},{32,64},{40,72},{48,80},{56,88},{64,... | collective-permute-start | bytes 835592 | tf_op jit(solution)/shard_map/ppermute | solution.py:46
  44.9 6.0 %collective-permute-start.3 = (f32[4,136,128]{2,1,0:T(8,128)S(1)}, f32[4,136,128]{2,1,0:T(8,128)S(1)}, u32[]{:S(2)}, u32[]{:S(2)}) collective-permute-start(f32[4,136,128]{2,1,0:T(8,128)S(1)} %maximum_maximum_fusion.1), channel_id=1, source_target_pairs={{0,96},{8,104},{16,112},{24,120},{32,128},{40,136},{48,144},{56,15... | collective-permute-start | bytes 835592 | tf_op jit(solution)/shard_map/ppermute | solution.py:46
  52.5 15.9 %collective-permute-done.4 = f32[4,136,128]{2,1,0:T(8,128)S(1)} collective-permute-done((f32[4,136,128]{2,1,0:T(8,128)S(1)}, f32[4,136,128]{2,1,0:T(8,128)S(1)}, u32[]{:S(2)}, u32[]{:S(2)}) %collective-permute-start.4) | collective-permute-done | bytes 278560 | tf_op jit(solution)/shard_map/ppermute | solution.py:46
  69.0 5.8 %collective-permute-start.6 = (f32[4,136,128]{2,1,0:T(8,128)S(1)}, f32[4,136,128]{2,1,0:T(8,128)S(1)}, u32[]{:S(2)}, u32[]{:S(2)}) collective-permute-start(f32[4,136,128]{2,1,0:T(8,128)S(1)} %maximum_maximum_fusion.2), channel_id=1, source_target_pairs={{0,128},{8,136},{16,144},{24,152},{32,160},{40,168},{48,176},{56,1... | collective-permute-start | bytes 835592 | tf_op jit(solution)/shard_map/ppermute | solution.py:46
  76.3 4.3 %collective-permute-done.6 = f32[4,136,128]{2,1,0:T(8,128)S(1)} collective-permute-done((f32[4,136,128]{2,1,0:T(8,128)S(1)}, f32[4,136,128]{2,1,0:T(8,128)S(1)}, u32[]{:S(2)}, u32[]{:S(2)}) %collective-permute-start.6) | collective-permute-done | bytes 278560 | tf_op jit(solution)/shard_map/ppermute | solution.py:46
  82.3 4.6 %convolution_bitcast_fusion = f32[8,256,384]{2,1,0:T(8,128)} fusion(bf16[256,512,1]{0,1,2:T(8,128)(2,1)S(1)} %bitcast.163, bf16[8,384,512]{2,1,0:T(8,128)(2,1)} %bitcast.162), kind=kOutput, calls=%fused_computation.21 | convolution fusion | flops 805306368 | bytes 6553600 | tf_op jit(solution)/shard_map/tk,gck->gtc/dot_general | solution.py:108
  87.6 45.2 %reduce-scatter.4.cloned.1.call-done = f32[1,256,384]{2,1,0:T(8,128)} async-done(((f32[8,256,384]{2,1,0:T(8,128)}), f32[1,256,384]{2,1,0:T(8,128)}) %reduce-scatter.4.cloned.1.call-update) | async-done | bytes 393232 | tf_op jit(solution)/shard_map/reduce_scatter | solution.py:109
  135.8 5.0 %all-to-all-start = ((bf16[8,264,384]{2,1,0:T(8,128)(2,1)}), bf16[8,264,384]{2,1,0:T(8,128)(2,1)S(1)}, u32[]{:S(2)}, u32[]{:S(2)}) async-start(bf16[8,264,384]{2,1,0:T(8,128)(2,1)} %stack.2), calls=%async_computation.1 | async-start | bytes 3244032 | tf_op jit(solution)/shard_map/all_to_all | solution.py:15
  148.3 30.8 %all-to-all-done = bf16[8,264,384]{2,1,0:T(8,128)(2,1)S(1)} async-done(((bf16[8,264,384]{2,1,0:T(8,128)(2,1)}), bf16[8,264,384]{2,1,0:T(8,128)(2,1)S(1)}, u32[]{:S(2)}, u32[]{:S(2)}) %all-to-all-start) | async-done | bytes 1622048 | tf_op jit(solution)/shard_map/all_to_all | solution.py:15
  180.3 5.0 %gather_fusion = bf16[768,3072]{1,0:T(8,128)(2,1)} fusion(bf16[256,3072]{1,0:T(8,128)(2,1)S(1)} %multiply_convert_fusion, s32[1024]{0:T(1024)S(1)} %pad_clamp_fusion.1), kind=kCustom, calls=%fused_computation | custom fusion | bytes 9440256 | tf_op jit(solution)/shard_map/gather | solution.py:140
  192.0 10.7 %all-to-all-start.3 = ((bf16[32,12,3072]{2,1,0:T(8,128)(2,1)}), bf16[32,12,3072]{2,1,0:T(8,128)(2,1)}, u32[]{:S(2)}, u32[]{:S(2)}) async-start(bf16[32,12,3072]{2,1,0:T(8,128)(2,1)} %get-tuple-element.66), calls=%async_computation.5 | async-start | bytes 6291456 | tf_op jit(solution)/shard_map/all_to_all | solution.py:147
  202.8 4.9 %copy.136 = bf16[80,8,8,384]{3,2,1,0:T(8,128)(2,1)} copy(bf16[80,8,8,384]{3,1,2,0:T(8,128)(2,1)} %bitcast.159) | data formatting | bytes 7864320
  207.7 34.8 %all-to-all-done.3 = bf16[32,12,3072]{2,1,0:T(8,128)(2,1)} async-done(((bf16[32,12,3072]{2,1,0:T(8,128)(2,1)}), bf16[32,12,3072]{2,1,0:T(8,128)(2,1)}, u32[]{:S(2)}, u32[]{:S(2)}) %all-to-all-start.3) | async-done | bytes 2359328 | tf_op jit(solution)/shard_map/all_to_all | solution.py:147
  242.5 4.2 %reshape.316 = bf16[384,3072]{1,0:T(8,128)(2,1)} reshape(bf16[32,12,3072]{2,1,0:T(8,128)(2,1)} %all-to-all-done.3) | data formatting | bytes 4718592 | tf_op jit(solution)/shard_map/reshape | solution.py:150
  246.8 4.8 %fusion.4 = f32[384,640]{1,0:T(8,128)S(1)} fusion(bf16[384,3072]{1,0:T(8,128)(2,1)} %reshape.316, bf16[1,3072,640]{2,1,0:T(8,128)(2,1)} %param.31), kind=kOutput, calls=%fused_computation.9 | convolution fusion | flops 1509949440 | bytes 7274496 | tf_op jit(solution)/shard_map/dot_general | solution.py:151
  251.6 10.3 %convert_bitcast_fusion.1 = bf16[8,384,384]{2,1,0:T(8,128)(2,1)} fusion(bf16[640,8,384]{2,1,0:T(8,128)(2,1)} %bitcast.160, bf16[384,3072]{1,0:T(8,128)(2,1)} %reshape.316, bf16[1,3072,640]{2,1,0:T(8,128)(2,1)} %param.32, f32[384,640]{1,0:T(8,128)S(1)} %fusion.4), kind=kOutput, calls=%fused_computation.19 | convolution fusion | flops 3022553088 | bytes 13565952 | tf_op jit(solution)/shard_map/rf,fgc->grc/dot_general | solution.py:154
  262.0 46.5 %all_to_all.25 = bf16[32,12,3072]{2,1,0:T(8,128)(2,1)} all-to-all(bf16[32,12,3072]{2,1,0:T(8,128)(2,1)} %get-tuple-element.65), channel_id=1, replica_groups=mesh['ctx'=32,'head'=8] {'ctx'}, dimensions={0} | all-to-all | bytes 4718592 | tf_op jit(solution)/shard_map/all_to_all | solution.py:147
  312.7 4.8 %fusion.6 = f32[384,640]{1,0:T(8,128)S(1)} fusion(bf16[384,3072]{1,0:T(8,128)(2,1)} %reshape.314, bf16[1,3072,640]{2,1,0:T(8,128)(2,1)} %param.31), kind=kOutput, calls=%fused_computation.11 | convolution fusion | flops 1509949440 | bytes 7274496 | tf_op jit(solution)/shard_map/dot_general | solution.py:151
  317.6 10.3 %convert_bitcast_fusion.2 = bf16[8,384,384]{2,1,0:T(8,128)(2,1)} fusion(bf16[640,8,384]{2,1,0:T(8,128)(2,1)} %bitcast.161, bf16[384,3072]{1,0:T(8,128)(2,1)} %reshape.314, bf16[1,3072,640]{2,1,0:T(8,128)(2,1)} %param.32, f32[384,640]{1,0:T(8,128)S(1)} %fusion.6), kind=kOutput, calls=%fused_computation.20 | convolution fusion | flops 3022553088 | bytes 13565952 | tf_op jit(solution)/shard_map/rf,fgc->grc/dot_general | solution.py:154
  334.3 25.5 %reduce-scatter.6.cloned.1.call-done = bf16[1,384,384]{2,1,0:T(8,128)(2,1)} async-done(((bf16[8,384,384]{2,1,0:T(8,128)(2,1)}), bf16[1,384,384]{2,1,0:T(8,128)(2,1)}) %reduce-scatter.6.cloned.1.call-update) | async-done | bytes 294928 | tf_op jit(solution)/shard_map/reduce_scatter | solution.py:157
  361.5 11.7 %all-to-all-start.2 = ((bf16[32,12,384]{2,1,0:T(8,128)(2,1)}), bf16[32,12,384]{2,1,0:T(8,128)(2,1)S(1)}, u32[]{:S(2)}, u32[]{:S(2)}) async-start(bf16[32,12,384]{2,1,0:T(8,128)(2,1)} %reshape.315), calls=%async_computation.4 | async-start | bytes 786432 | tf_op jit(solution)/shard_map/all_to_all | solution.py:159
  373.5 9.9 %all-to-all-done.2 = bf16[32,12,384]{2,1,0:T(8,128)(2,1)S(1)} async-done(((bf16[32,12,384]{2,1,0:T(8,128)(2,1)}), bf16[32,12,384]{2,1,0:T(8,128)(2,1)S(1)}, u32[]{:S(2)}, u32[]{:S(2)}) %all-to-all-start.2) | async-done | bytes 294944 | tf_op jit(solution)/shard_map/all_to_all | solution.py:159
  (135 shorter events, 61.8 us)
Async XLA Ops:
  6.5 44.4 %copy-start = (bf16[256,512]{1,0:T(8,128)(2,1)S(1)}, bf16[256,512]{1,0:T(8,128)(2,1)}, u32[]{:S(2)}) copy-start(bf16[256,512]{1,0:T(8,128)(2,1)} %param.21) | copy-start | bytes 786436
  6.5 44.5 %copy-start.5 = (bf16[256,512]{1,0:T(8,128)(2,1)S(1)}, bf16[256,512]{1,0:T(8,128)(2,1)}, u32[]{:S(2)}) copy-start(bf16[256,512]{1,0:T(8,128)(2,1)} %param.23) | copy-start | bytes 786436
  6.5 75.8 %all-gather.2.cloned.1.call-start = ((), (), s32[]{:S(2)}) async-start(), calls=%async_computation.8 | async-start | bytes 3244032 | tf_op jit(solution)/shard_map/all_gather | solution.py:105
  7.3 125.6 %reduce-scatter.4.cloned.1.call-start = ((), (), s32[]{:S(2)}) async-start(), calls=%async_computation.9 | async-start | bytes 3538944 | tf_op jit(solution)/shard_map/reduce_scatter | solution.py:109
  10.8 25.5 %copy-start.10 = (f32[136]{0:T(256)}, f32[136]{0:T(256)S(1)}, u32[]{:S(2)}) copy-start(f32[136]{0:T(256)S(1)} %pad.23.clone) | copy-start | bytes 1636
  13.1 11.2 %collective-permute-start.2 = (f32[4,136,128]{2,1,0:T(8,128)S(1)}, f32[4,136,128]{2,1,0:T(8,128)S(1)}, u32[]{:S(2)}, u32[]{:S(2)}) collective-permute-start(f32[4,136,128]{2,1,0:T(8,128)S(1)} %maximum_maximum_fusion), channel_id=1, source_target_pairs={{0,24},{8,32},{16,40},{24,48},{32,56},{40,64},{48,72},{56,80},{64,... | collective-permute-start | bytes 835592 | tf_op jit(solution)/shard_map/ppermute | solution.py:46
  19.2 11.2 %collective-permute-start.1 = (f32[4,136,128]{2,1,0:T(8,128)S(1)}, f32[4,136,128]{2,1,0:T(8,128)S(1)}, u32[]{:S(2)}, u32[]{:S(2)}) collective-permute-start(f32[4,136,128]{2,1,0:T(8,128)S(1)} %maximum_maximum_fusion), channel_id=1, source_target_pairs={{0,8},{8,16},{16,24},{24,32},{32,40},{40,48},{48,56},{56,64},{64,7... | collective-permute-start | bytes 835592 | tf_op jit(solution)/shard_map/ppermute | solution.py:46
  21.1 13.3 %collective-permute-start = (f32[4,136,128]{2,1,0:T(8,128)S(1)}, f32[4,136,128]{2,1,0:T(8,128)S(1)}, u32[]{:S(2)}, u32[]{:S(2)}) collective-permute-start(f32[4,136,128]{2,1,0:T(8,128)S(1)} %maximum_maximum_fusion), channel_id=1, source_target_pairs={{0,16},{8,24},{16,32},{24,40},{32,48},{40,56},{48,64},{56,72},{64,... | collective-permute-start | bytes 835592 | tf_op jit(solution)/shard_map/ppermute | solution.py:46
  35.4 33.0 %copy-start.2 = (f32[4,136,128]{2,1,0:T(8,128)S(1)}, f32[4,136,128]{2,1,0:T(8,128)}, u32[]{:S(2)}) copy-start(f32[4,136,128]{2,1,0:T(8,128)} %constant.174.clone.1) | copy-start | bytes 835588
  36.0 8.9 %copy-start.7 = (f32[4,1,128]{2,1,0:T(1,128)}, f32[4,1,128]{2,1,0:T(1,128)S(1)}, u32[]{:S(2)}) copy-start(f32[4,1,128]{2,1,0:T(1,128)S(1)} %get-tuple-element.62) | copy-start | bytes 6148
  36.4 16.2 %collective-permute-start.5 = (f32[4,136,128]{2,1,0:T(8,128)S(1)}, f32[4,136,128]{2,1,0:T(8,128)S(1)}, u32[]{:S(2)}, u32[]{:S(2)}) collective-permute-start(f32[4,136,128]{2,1,0:T(8,128)S(1)} %maximum_maximum_fusion.1), channel_id=1, source_target_pairs={{0,32},{8,40},{16,48},{24,56},{32,64},{40,72},{48,80},{56,88},{64,... | collective-permute-start | bytes 835592 | tf_op jit(solution)/shard_map/ppermute | solution.py:46
  41.7 26.7 %collective-permute-start.4 = (f32[4,136,128]{2,1,0:T(8,128)S(1)}, f32[4,136,128]{2,1,0:T(8,128)S(1)}, u32[]{:S(2)}, u32[]{:S(2)}) collective-permute-start(f32[4,136,128]{2,1,0:T(8,128)S(1)} %maximum_maximum_fusion.1), channel_id=1, source_target_pairs={{0,64},{8,72},{16,80},{24,88},{32,96},{40,104},{48,112},{56,120},{... | collective-permute-start | bytes 835592 | tf_op jit(solution)/shard_map/ppermute | solution.py:46
  44.9 23.5 %collective-permute-start.3 = (f32[4,136,128]{2,1,0:T(8,128)S(1)}, f32[4,136,128]{2,1,0:T(8,128)S(1)}, u32[]{:S(2)}, u32[]{:S(2)}) collective-permute-start(f32[4,136,128]{2,1,0:T(8,128)S(1)} %maximum_maximum_fusion.1), channel_id=1, source_target_pairs={{0,96},{8,104},{16,112},{24,120},{32,128},{40,136},{48,144},{56,15... | collective-permute-start | bytes 835592 | tf_op jit(solution)/shard_map/ppermute | solution.py:46
  52.4 16.5 %copy-start.11 = (f32[136]{0:T(256)S(1)}, f32[136]{0:T(256)}, u32[]{:S(2)}) copy-start(f32[136]{0:T(256)} %copy-done.10) | copy-start | bytes 1636
  69.0 11.6 %collective-permute-start.6 = (f32[4,136,128]{2,1,0:T(8,128)S(1)}, f32[4,136,128]{2,1,0:T(8,128)S(1)}, u32[]{:S(2)}, u32[]{:S(2)}) collective-permute-start(f32[4,136,128]{2,1,0:T(8,128)S(1)} %maximum_maximum_fusion.2), channel_id=1, source_target_pairs={{0,128},{8,136},{16,144},{24,152},{32,160},{40,168},{48,176},{56,1... | collective-permute-start | bytes 835592 | tf_op jit(solution)/shard_map/ppermute | solution.py:46
  87.0 45.9 %copy-start.4 = (bf16[256,384]{1,0:T(8,128)(2,1)S(1)}, bf16[256,384]{1,0:T(8,128)(2,1)}, u32[]{:S(2)}) copy-start(bf16[256,384]{1,0:T(8,128)(2,1)} %param.27) | copy-start | bytes 589828
  87.6 53.2 %copy-start.9 = (s32[256,2]{0,1:T(2,128)S(1)}, s32[256,2]{0,1:T(2,128)}, u32[]{:S(2)}) copy-start(s32[256,2]{0,1:T(2,128)} %param.30) | copy-start | bytes 6148
  135.8 43.3 %all-to-all-start = ((bf16[8,264,384]{2,1,0:T(8,128)(2,1)}), bf16[8,264,384]{2,1,0:T(8,128)(2,1)S(1)}, u32[]{:S(2)}, u32[]{:S(2)}) async-start(bf16[8,264,384]{2,1,0:T(8,128)(2,1)} %stack.2), calls=%async_computation.1 | async-start | bytes 3244032 | tf_op jit(solution)/shard_map/all_to_all | solution.py:15
  192.0 50.5 %all-to-all-start.3 = ((bf16[32,12,3072]{2,1,0:T(8,128)(2,1)}), bf16[32,12,3072]{2,1,0:T(8,128)(2,1)}, u32[]{:S(2)}, u32[]{:S(2)}) async-start(bf16[32,12,3072]{2,1,0:T(8,128)(2,1)} %get-tuple-element.66), calls=%async_computation.5 | async-start | bytes 6291456 | tf_op jit(solution)/shard_map/all_to_all | solution.py:147
  202.7 125.2 %reduce-scatter.8.cloned.1.call-start = ((), (), s32[]{:S(2)}) async-start(), calls=%async_computation.11 | async-start | bytes 2654208 | tf_op jit(solution)/shard_map/reduce_scatter | solution.py:157
  261.9 97.8 %reduce-scatter.6.cloned.1.call-start = ((), (), s32[]{:S(2)}) async-start(), calls=%async_computation.10 | async-start | bytes 2654208 | tf_op jit(solution)/shard_map/reduce_scatter | solution.py:157
  327.9 5.8 %copy-start.6 = (bf16[3072,32]{0,1:T(8,128)(2,1)S(1)}, bf16[3072,32]{0,1:T(8,128)(2,1)}, u32[]{:S(2)}) copy-start(bf16[3072,32]{0,1:T(8,128)(2,1)} %param.29) | copy-start | bytes 589828
  329.7 31.8 %all-to-all-start.4 = ((bf16[32,12,384]{2,1,0:T(8,128)(2,1)}), bf16[32,12,384]{2,1,0:T(8,128)(2,1)S(1)}, u32[]{:S(2)}, u32[]{:S(2)}) async-start(bf16[32,12,384]{2,1,0:T(8,128)(2,1)} %reshape.317), calls=%async_computation.7 | async-start | bytes 786432 | tf_op jit(solution)/shard_map/all_to_all | solution.py:159
  361.5 21.9 %all-to-all-start.2 = ((bf16[32,12,384]{2,1,0:T(8,128)(2,1)}), bf16[32,12,384]{2,1,0:T(8,128)(2,1)S(1)}, u32[]{:S(2)}, u32[]{:S(2)}) async-start(bf16[32,12,384]{2,1,0:T(8,128)(2,1)} %reshape.315), calls=%async_computation.4 | async-start | bytes 786432 | tf_op jit(solution)/shard_map/all_to_all | solution.py:159
  (5 other events, 13.0 us)
Sparse Core Ops, SparseCore 0:
  9.9 61.5 all-gather.1
  87.1 45.7 reduce-scatter.3
  262.0 32.7 reduce-scatter.7
  328.0 31.6 reduce-scatter.5
